TPU v7x, 256 devices: a whole 4x4x8 slice. The times are simulated.
256 devices in a mesh: panel: 2 (over z_lo), wide: 32 (over y, z_hi, core), narrow: 4 (over x).
Axes of the slice: x: 4, y: 4, z: 8 (z_hi: 4, z_lo: 2; z = z_hi * 2 + z_lo), core: 2. Of those that a mesh axis runs over, the one named last changes fastest.
Arguments:
- heat_scalar: float32 [2, 64, 1536, 512], P('panel', None, 'wide', 'narrow'), may hold values from -6 to 6
- polar_flow_speed: bfloat16 [2, 64, 1536, 512], P('panel', None, 'wide', 'narrow'), may hold values from -4 to 4
- azimuthal_flow_speed: bfloat16 [2, 64, 1536, 512], P('panel', None, 'wide', 'narrow'), may hold values from -4 to 4
- conduction_coefficient: float32 [2, 64, 1536, 512], P('panel', None, 'wide', 'narrow'), may hold values from 0.01 to 0.1
- interpolant_anchor_position: int32 [2, 4, 32, 64], P('panel', 'narrow', 'wide'), may hold values from 0 to 6143
- interpolant_factors: float32 [2, 4, 32, 2, 64], P('panel', 'narrow', 'wide'), may hold values from 0 to 1
- boundary_source_slot: int32 [2, 4, 32, 352], P('panel', 'narrow', 'wide'), may hold values from -1 to 8191, as said below
Outputs:
- temperature_next: float32 [2, 64, 1536, 512], P('panel', None, 'wide', 'narrow')
Inputs may be any that keep to these rules, and one draw needn't show every extreme that they name: `boundary_source_slot`: entries are d * 64 + e, naming entry e of the donor tile with wide index d // 4 and narrow index d % 4 of the other panel; exactly the rim cells that lie outside the panel carry such an entry, the others -1; each donor entry fills at most one cell, a tile's used entries are its first ones, every tile uses at most 64 entries and some tile exactly 64; all but at most one of the tiles that use any entry use 3 * 16 or more.
All inputs are finite; a program needn't handle non-finite values.
Results may differ from a plain program's by a relative error of at most 0.0003.
Values sent between devices are 32-bit elements; how exact they have to be, the bound alone decides.
No kernel may reach another device: no remote copies, remote signals or barrier semaphores. Data moves between devices by JAX's collectives and lax.ppermute only.
A program may use at most 128 MiB of HBM per device.

v0:
```python
import math

import jax
import jax.numpy as jnp
from jax import lax
from jax.sharding import PartitionSpec as P

TIME_INCREMENT = 0.5
MARGIN = 0.04


def extended_2(shard, sides, width):
    for axis, dim in sides:
        peers, length = (lax.axis_size(axis), shard.shape[dim])
        up = [(i, (i + 1) % peers) for i in range(peers - 1)]
        down = [(j, i) for i, j in up]
        last = lax.slice_in_dim(shard, length - width, length, axis=dim)
        leading = lax.slice_in_dim(shard, 0, width, axis=dim)
        before = lax.ppermute(last, axis, up)
        after = lax.ppermute(leading, axis, down)
        shard = jnp.concatenate([before, shard, after], axis=dim)
    return shard


def swapped(shard, axis, bit):
    return lax.ppermute(shard, axis, [(i, i ^ 1 << bit) for i in range(lax.axis_size(axis))])


def inverse_metrics(level_values, row_values, total_rows, level_count):
    radius = 0.55 + 0.45 * (level_values + 0.5) / level_count
    angle_span = 0.5 * math.pi + 2.0 * MARGIN
    colatitude = 0.25 * math.pi - MARGIN + (row_values + 0.5) * angle_span / total_rows
    return (1.0 / radius, 1.0 / jnp.sin(colatitude))


def horizontal(extended, k_extended, speed_theta, speed_phi, radius_inv, sine_inv):
    centre = extended[..., 1:-1, 1:-1]
    upper_cell = extended[..., 1:-1, :-2]
    lower_cell = extended[..., 1:-1, 2:]
    west_cell = extended[..., :-2, 1:-1]
    east_cell = extended[..., 2:, 1:-1]
    k_centre = k_extended[..., 1:-1, 1:-1]
    k_upper = jnp.maximum(k_extended[..., 1:-1, :-2], k_centre)
    k_lower = jnp.maximum(k_extended[..., 1:-1, 2:], k_centre)
    k_west = jnp.maximum(k_extended[..., :-2, 1:-1], k_centre)
    k_east = jnp.maximum(k_extended[..., 2:, 1:-1], k_centre)
    transport = (
        -0.5
        * radius_inv
        * (speed_theta * (lower_cell - upper_cell) + speed_phi * sine_inv * (east_cell - west_cell))
    )
    spread_terms = (
        radius_inv
        * radius_inv
        * (
            k_lower * (lower_cell - centre)
            - k_upper * (centre - upper_cell)
            + sine_inv * sine_inv * (k_east * (east_cell - centre) - k_west * (centre - west_cell))
        )
    )
    return transport + spread_terms


def radial(centre, k_centre):
    k_faces = 0.5 * (k_centre[1:] + k_centre[:-1])
    fluxes = k_faces * (centre[1:] - centre[:-1])
    zero_face = jnp.zeros_like(centre[:1])
    return jnp.concatenate([fluxes, zero_face], axis=0) - jnp.concatenate(
        [zero_face, fluxes], axis=0
    )


def shards(
    heat_scalar,
    polar_flow_speed,
    azimuthal_flow_speed,
    conduction_coefficient,
    interpolant_anchor_position,
    interpolant_factors,
    boundary_source_slot,
):
    current_state = heat_scalar[0]
    level_count, col_count, row_count = current_state.shape
    speed_theta = polar_flow_speed[0].astype(jnp.float32)
    speed_phi = azimuthal_flow_speed[0].astype(jnp.float32)
    k_local = conduction_coefficient[0]
    k_ext = extended_2(k_local, (("wide", 1), ("narrow", 2)), 1)
    row_global = lax.axis_index("narrow") * row_count + jnp.arange(row_count, dtype=jnp.int32)
    radius_inv, sine_inv = inverse_metrics(
        jnp.arange(level_count, dtype=jnp.float32),
        row_global.astype(jnp.float32),
        row_count * lax.axis_size("narrow"),
        level_count,
    )
    radius_inv = radius_inv[:, None, None]
    sine_inv = sine_inv[None, None, :]
    cells = interpolant_anchor_position[0, 0, 0]
    weight_a = interpolant_factors[0, 0, 0, 0]
    weight_b = interpolant_factors[0, 0, 0, 1]
    sources = boundary_source_slot[0, 0, 0]
    capacity = cells.shape[0]
    row_width = row_count + 2
    base_index = (cells // row_count + 1) * row_width + cells % row_count + 1

    def picker(offset, piece):
        count = piece.shape[0]
        target = sources + offset
        donor_row = target // capacity
        donor_entry = target % capacity
        usable = (sources >= 0) & (donor_row >= 0) & (donor_row < count)
        received = piece[jnp.clip(donor_row, 0, count - 1), :, donor_entry]
        return jnp.where(usable[:, None], received, jnp.zeros_like(received))

    def donor_ghosts(extended):
        flattened = extended.reshape(level_count, -1)
        values = (
            (1.0 - weight_a) * (1.0 - weight_b) * jnp.take(flattened, base_index, axis=1)
            + weight_a * (1.0 - weight_b) * jnp.take(flattened, base_index + 1, axis=1)
            + (1.0 - weight_a) * weight_b * jnp.take(flattened, base_index + row_width, axis=1)
            + weight_a * weight_b * jnp.take(flattened, base_index + row_width + 1, axis=1)
        )
        crossed = swapped(values, "panel", 0)
        total = picker(0, lax.all_gather(crossed[None], ("wide", "narrow"), axis=0, tiled=True))
        return total.T

    def split_rim(ghosts):
        upper_rim = ghosts[:, :col_count]
        lower_rim = ghosts[:, col_count : 2 * col_count]
        west_rim = ghosts[:, 2 * col_count : 2 * col_count + row_count]
        east_rim = ghosts[:, 2 * col_count + row_count :]
        return (upper_rim, lower_rim, west_rim, east_rim)

    def tendency(extended):
        return horizontal(extended, k_ext, speed_theta, speed_phi, radius_inv, sine_inv) + radial(
            extended[:, 1:-1, 1:-1], k_local
        )

    def with_rim(extended, ghosts):
        upper_rim, lower_rim, west_rim, east_rim = split_rim(ghosts)
        extended = extended.at[:, 1:-1, 0].add(upper_rim).at[:, 1:-1, -1].add(lower_rim)
        return extended.at[:, 0, 1:-1].add(west_rim).at[:, -1, 1:-1].add(east_rim)

    def evaluate_derivative(current):
        extended = extended_2(current, (("wide", 1), ("narrow", 2)), 1)
        ghosts = donor_ghosts(extended)
        return tendency(with_rim(extended, ghosts))

    predictor_state = current_state + TIME_INCREMENT * evaluate_derivative(current_state)
    result = 0.5 * (
        current_state + predictor_state + TIME_INCREMENT * evaluate_derivative(predictor_state)
    )
    return result[None]


def solution(mesh):
    placed = (
        P("panel", None, "wide", "narrow"),
        P("panel", None, "wide", "narrow"),
        P("panel", None, "wide", "narrow"),
        P("panel", None, "wide", "narrow"),
        P("panel", "narrow", "wide", None),
        P("panel", "narrow", "wide", None, None),
        P("panel", "narrow", "wide", None),
    )
    return jax.shard_map(
        shards,
        mesh=mesh,
        in_specs=placed,
        out_specs=P("panel", None, "wide", "narrow"),
        check_vma=False,
    )
```

profile of v0, /device:TPU:1, one launch (start us, length us, event | category | flops | bytes accessed | tf_op | source)
XLA Modules:
  0.0 365.9 jit_solution(10578066881099782307)
XLA Ops:
  8.7 6.3 %collective-permute-start = (f32[64,1,128]{0,2,1:T(8,128)S(1)}, f32[64,1,128]{0,2,1:T(8,128)S(1)}, u32[]{:S(2)}, u32[]{:S(2)}) collective-permute-start(f32[64,1,128]{0,2,1:T(8,128)S(1)} %get-tuple-element.121), channel_id=1, source_target_pairs={{0,4},{4,8},{8,12},{12,16},{16,20},{20,24},{24,28},{28,32},{32,36}... | collective-permute-start | bytes 98312 | tf_op jit(solution)/shard_map/ppermute | solution.py:19
  38.5 3.2 gather_fusion.2
  41.8 3.1 gather_fusion.5
  49.7 3.3 copy.57
  54.5 5.1 %collective-permute-start.5 = (f32[64,1,128]{0,2,1:T(8,128)}, f32[64,1,128]{0,2,1:T(8,128)S(1)}, u32[]{:S(2)}, u32[]{:S(2)}) collective-permute-start(f32[64,1,128]{0,2,1:T(8,128)} %get-tuple-element.119), channel_id=1, source_target_pairs={{0,4},{4,8},{8,12},{12,16},{16,20},{20,24},{24,28},{28,32},{32,36}... | collective-permute-start | bytes 98312 | tf_op jit(solution)/shard_map/ppermute | solution.py:19
  71.4 3.7 %collective-permute-start.8 = (f32[64,50,1]{0,2,1:T(1,128)}, f32[64,50,1]{0,2,1:T(1,128)}, u32[]{:S(2)}, u32[]{:S(2)}) collective-permute-start(f32[64,50,1]{0,2,1:T(1,128)} %get-tuple-element.113), channel_id=1, source_target_pairs={{0,1},{1,2},{2,3},{4,5},{5,6},{6,7},{8,9},{9,10},{10,11},{12,13},{... | collective-permute-start | bytes 38408 | tf_op jit(solution)/shard_map/ppermute | solution.py:19
  76.4 56.3 %all-gather.5.cloned.1.call-done = f32[8192,64]{1,0:T(8,128)} async-done(((f32[64,64]{1,0:T(8,128)}), f32[8192,64]{1,0:T(8,128)}) %all-gather.5.cloned.1.call-update) | async-done | bytes 2097168 | tf_op jit(solution)/shard_map/all_gather | solution.py:123
  132.8 5.7 %copy.55 = f32[128,64,64]{1,2,0:T(8,128)} copy(f32[128,64,64]{2,1,0:T(8,128)} %bitcast.153) | data formatting | bytes 4194304 | tf_op jit(solution)/shard_map/all_gather | solution.py:123
  138.5 17.4 %gather_fusion = f32[352,64]{1,0:T(8,128)} fusion(f32[128,64,64]{1,2,0:T(8,128)} %copy.55, s32[352]{0:T(512)S(1)} %fusion.43), kind=kCustom, calls=%fused_computation.8 | custom fusion | bytes 183040 | tf_op jit(solution)/shard_map/gather | solution.py:111
  169.8 4.7 %fusion.15 = f32[63,48,128]{0,2,1:T(8,128)S(1)} fusion(f32[64,50,130]{0,2,1:T(8,128)S(1)} %scatter-add.31, f32[1,64,48,128]{1,3,2,0:T(8,128)} %copy.57), kind=kLoop, calls=%fused_computation.31 | loop fusion | flops 1548288 | bytes 7741440 | tf_op jit(solution)/shard_map/mul | solution.py:66
  175.3 8.7 %fusion.5 = f32[64,48,128]{0,2,1:T(8,128)S(1)} fusion(f32[63,48,128]{0,2,1:T(8,128)S(1)} %fusion.15, f32[64,50,130]{0,2,1:T(8,128)S(1)} %scatter-add.31, f32[64,48,128]{0,2,1:T(8,128)S(1)} %bitcast.148, f32[64,1,128]{0,2,1:T(8,128)} %collective-permute-done.6, f32[64,1,128]{0,2,1:T(8,128)S(1)} %collective-permute-done.5, ...), kind=kLoop, calls=%fused_computation.19 | loop fusion | flops 15335424 | bytes 15796736 | tf_op jit(solution)/shard_map/add | solution.py:148
  184.0 3.4 collective-permute-start.9
  189.4 5.2 %collective-permute-done.10 = f32[64,1,128]{0,2,1:T(8,128)S(1)} collective-permute-done((f32[64,1,128]{0,2,1:T(8,128)S(1)}, f32[64,1,128]{0,2,1:T(8,128)S(1)}, u32[]{:S(2)}, u32[]{:S(2)}) %collective-permute-start.10) | collective-permute-done | bytes 32800 | tf_op jit(solution)/shard_map/ppermute | solution.py:20
  194.7 4.0 %collective-permute-start.11 = (f32[64,50,1]{0,1,2:T(8,128)S(1)}, f32[64,50,1]{0,1,2:T(8,128)S(1)}, u32[]{:S(2)}, u32[]{:S(2)}) collective-permute-start(f32[64,50,1]{0,1,2:T(8,128)S(1)} %copy.80), channel_id=1, source_target_pairs={{0,1},{1,2},{2,3},{4,5},{5,6},{6,7},{8,9},{9,10},{10,11},{12,13},{... | collective-permute-start | bytes 38408 | tf_op jit(solution)/shard_map/ppermute | solution.py:19
  205.7 3.2 gather_fusion.8
  209.0 3.2 gather_fusion.7
  212.2 3.3 gather_fusion.6
  215.5 3.2 gather_fusion.9
  224.1 79.1 %all-gather.7.cloned.1.call-done = f32[8192,64]{1,0:T(8,128)} async-done(((f32[64,64]{1,0:T(8,128)}), f32[8192,64]{1,0:T(8,128)}) %all-gather.7.cloned.1.call-update) | async-done | bytes 2097168 | tf_op jit(solution)/shard_map/all_gather | solution.py:123
  303.2 5.7 %copy.69 = f32[128,64,64]{1,2,0:T(8,128)} copy(f32[128,64,64]{2,1,0:T(8,128)} %bitcast.154) | data formatting | bytes 4194304 | tf_op jit(solution)/shard_map/all_gather | solution.py:123
  309.0 17.4 %gather_fusion.1 = f32[352,64]{1,0:T(8,128)} fusion(f32[128,64,64]{1,2,0:T(8,128)} %copy.69, s32[352]{0:T(512)S(1)} %fusion.43), kind=kCustom, calls=%fused_computation.9 | custom fusion | bytes 183040 | tf_op jit(solution)/shard_map/gather | solution.py:111
  339.7 4.7 %fusion.14 = f32[63,48,128]{0,2,1:T(8,128)S(1)} fusion(f32[64,50,130]{0,2,1:T(8,128)S(1)} %scatter-add.39, f32[1,64,48,128]{1,3,2,0:T(8,128)} %copy.57), kind=kLoop, calls=%fused_computation.29 | loop fusion | flops 1548288 | bytes 7741440 | tf_op jit(solution)/shard_map/mul | solution.py:66
  346.1 9.8 %fusion.13 = f32[1,64,48,128]{1,3,2,0:T(8,128)} fusion(f32[63,48,128]{0,2,1:T(8,128)S(1)} %fusion.14, f32[64,50,130]{0,2,1:T(8,128)S(1)} %scatter-add.39, f32[64,48,128]{0,2,1:T(8,128)S(1)} %copy-done.6, f32[64,48,128]{0,2,1:T(8,128)S(1)} %bitcast.149, f32[64,1,128]{0,2,1:T(8,128)} %collective-permute-done.6, f32[64,1,128]{0,2,1:T(8,128)S(1)} %collective-permute-done.5, ...), kind=kLoop, calls=%fused_computation.27 | loop fusion | flops 16121856 | bytes 17369600 | tf_op jit(solution)/shard_map/broadcast_in_dim | solution.py:152
  355.9 3.2 copy.73
  (144 shorter events, 88.7 us)
Async XLA Ops:
  6.5 126.2 %all-gather.5.cloned.1.call-start = ((), (), s32[]{:S(2)}) async-start(), calls=%async_computation | async-start | bytes 4227072 | tf_op jit(solution)/shard_map/all_gather | solution.py:123
  8.7 17.9 %copy-start.2 = (f32[1,64,48,128]{1,3,2,0:T(8,128)}, f32[1,64,48,128]{1,3,2,0:T(8,128)S(1)}, u32[]{:S(2)}) copy-start(f32[1,64,48,128]{1,3,2,0:T(8,128)S(1)} %copy.46) | copy-start | bytes 4718596
  8.7 10.0 %collective-permute-start = (f32[64,1,128]{0,2,1:T(8,128)S(1)}, f32[64,1,128]{0,2,1:T(8,128)S(1)}, u32[]{:S(2)}, u32[]{:S(2)}) collective-permute-start(f32[64,1,128]{0,2,1:T(8,128)S(1)} %get-tuple-element.121), channel_id=1, source_target_pairs={{0,4},{4,8},{8,12},{12,16},{16,20},{20,24},{24,28},{28,32},{32,36}... | collective-permute-start | bytes 98312 | tf_op jit(solution)/shard_map/ppermute | solution.py:19
  15.0 6.5 %collective-permute-start.1 = (f32[64,1,128]{0,2,1:T(8,128)S(1)}, f32[64,1,128]{0,2,1:T(8,128)S(1)}, u32[]{:S(2)}, u32[]{:S(2)}) collective-permute-start(f32[64,1,128]{0,2,1:T(8,128)S(1)} %get-tuple-element.122), channel_id=1, source_target_pairs={{4,0},{8,4},{12,8},{16,12},{20,16},{24,20},{28,24},{32,28},{36,32}... | collective-permute-start | bytes 98312 | tf_op jit(solution)/shard_map/ppermute | solution.py:20
  18.7 14.8 %copy-start.16 = (s32[1024]{0:T(1024)}, s32[1024]{0:T(1024)S(1)}, u32[]{:S(2)}) copy-start(s32[1024]{0:T(1024)S(1)} %get-tuple-element.136) | copy-start | bytes 12292
  18.7 23.1 %copy-start.15 = (s32[1024]{0:T(1024)}, s32[1024]{0:T(1024)S(1)}, u32[]{:S(2)}) copy-start(s32[1024]{0:T(1024)S(1)} %get-tuple-element.135) | copy-start | bytes 12292
  18.7 17.3 %copy-start.17 = (s32[1024]{0:T(1024)}, s32[1024]{0:T(1024)S(1)}, u32[]{:S(2)}) copy-start(s32[1024]{0:T(1024)S(1)} %pad_clamp_fusion.2) | copy-start | bytes 12292
  21.5 5.0 %collective-permute-start.2 = (f32[64,50,1]{0,2,1:T(1,128)S(1)}, f32[64,50,1]{0,2,1:T(1,128)S(1)}, u32[]{:S(2)}, u32[]{:S(2)}) collective-permute-start(f32[64,50,1]{0,2,1:T(1,128)S(1)} %get-tuple-element.115), channel_id=1, source_target_pairs={{0,1},{1,2},{2,3},{4,5},{5,6},{6,7},{8,9},{9,10},{10,11},{12,13},{... | collective-permute-start | bytes 38408 | tf_op jit(solution)/shard_map/ppermute | solution.py:19
  24.7 4.6 %collective-permute-start.3 = (f32[64,50,1]{0,2,1:T(1,128)S(1)}, f32[64,50,1]{0,2,1:T(1,128)S(1)}, u32[]{:S(2)}, u32[]{:S(2)}) collective-permute-start(f32[64,50,1]{0,2,1:T(1,128)S(1)} %get-tuple-element.116), channel_id=1, source_target_pairs={{1,0},{2,1},{3,2},{5,4},{6,5},{7,6},{9,8},{10,9},{11,10},{13,12},{... | collective-permute-start | bytes 38408 | tf_op jit(solution)/shard_map/ppermute | solution.py:20
  45.9 3.0 collective-permute-start.4
  49.6 253.6 %all-gather.7.cloned.1.call-start = ((), (), s32[]{:S(2)}) async-start(), calls=%async_computation.1 | async-start | bytes 4227072 | tf_op jit(solution)/shard_map/all_gather | solution.py:123
  54.5 15.2 %collective-permute-start.5 = (f32[64,1,128]{0,2,1:T(8,128)}, f32[64,1,128]{0,2,1:T(8,128)S(1)}, u32[]{:S(2)}, u32[]{:S(2)}) collective-permute-start(f32[64,1,128]{0,2,1:T(8,128)} %get-tuple-element.119), channel_id=1, source_target_pairs={{0,4},{4,8},{8,12},{12,16},{16,20},{20,24},{24,28},{28,32},{32,36}... | collective-permute-start | bytes 98312 | tf_op jit(solution)/shard_map/ppermute | solution.py:19
  59.6 10.2 %collective-permute-start.6 = (f32[64,1,128]{0,2,1:T(8,128)}, f32[64,1,128]{0,2,1:T(8,128)}, u32[]{:S(2)}, u32[]{:S(2)}) collective-permute-start(f32[64,1,128]{0,2,1:T(8,128)} %get-tuple-element.120), channel_id=1, source_target_pairs={{4,0},{8,4},{12,8},{16,12},{20,16},{24,20},{28,24},{32,28},{36,32}... | collective-permute-start | bytes 98312 | tf_op jit(solution)/shard_map/ppermute | solution.py:20
  71.4 103.1 %collective-permute-start.8 = (f32[64,50,1]{0,2,1:T(1,128)}, f32[64,50,1]{0,2,1:T(1,128)}, u32[]{:S(2)}, u32[]{:S(2)}) collective-permute-start(f32[64,50,1]{0,2,1:T(1,128)} %get-tuple-element.113), channel_id=1, source_target_pairs={{0,1},{1,2},{2,3},{4,5},{5,6},{6,7},{8,9},{9,10},{10,11},{12,13},{... | collective-permute-start | bytes 38408 | tf_op jit(solution)/shard_map/ppermute | solution.py:19
  75.1 99.4 %collective-permute-start.7 = (f32[64,50,1]{0,2,1:T(1,128)}, f32[64,50,1]{0,2,1:T(1,128)}, u32[]{:S(2)}, u32[]{:S(2)}) collective-permute-start(f32[64,50,1]{0,2,1:T(1,128)} %get-tuple-element.114), channel_id=1, source_target_pairs={{1,0},{2,1},{3,2},{5,4},{6,5},{7,6},{9,8},{10,9},{11,10},{13,12},{... | collective-permute-start | bytes 38408 | tf_op jit(solution)/shard_map/ppermute | solution.py:20
  132.8 23.2 %copy-start.20 = (pred[352]{0:T(512)(128)(4,1)S(1)}, pred[352]{0:T(512)(128)(4,1)}, u32[]{:S(2)}) copy-start(pred[352]{0:T(512)(128)(4,1)} %compare_and_fusion.4) | copy-start | bytes 1060
  184.0 19.3 %copy-start.5 = (f32[64,48,128]{0,2,1:T(8,128)}, f32[64,48,128]{0,2,1:T(8,128)S(1)}, u32[]{:S(2)}) copy-start(f32[64,48,128]{0,2,1:T(8,128)S(1)} %fusion.5) | copy-start | bytes 4718596
  184.0 5.3 %collective-permute-start.9 = (f32[64,1,128]{0,2,1:T(8,128)S(1)}, f32[64,1,128]{0,2,1:T(8,128)S(1)}, u32[]{:S(2)}, u32[]{:S(2)}) collective-permute-start(f32[64,1,128]{0,2,1:T(8,128)S(1)} %get-tuple-element.117), channel_id=1, source_target_pairs={{0,4},{4,8},{8,12},{12,16},{16,20},{20,24},{24,28},{28,32},{32,36}... | collective-permute-start | bytes 98312 | tf_op jit(solution)/shard_map/ppermute | solution.py:19
  187.4 7.2 %collective-permute-start.10 = (f32[64,1,128]{0,2,1:T(8,128)S(1)}, f32[64,1,128]{0,2,1:T(8,128)S(1)}, u32[]{:S(2)}, u32[]{:S(2)}) collective-permute-start(f32[64,1,128]{0,2,1:T(8,128)S(1)} %get-tuple-element.118), channel_id=1, source_target_pairs={{4,0},{8,4},{12,8},{16,12},{20,16},{24,20},{28,24},{32,28},{36,32}... | collective-permute-start | bytes 98312 | tf_op jit(solution)/shard_map/ppermute | solution.py:20
  194.7 5.5 %collective-permute-start.11 = (f32[64,50,1]{0,1,2:T(8,128)S(1)}, f32[64,50,1]{0,1,2:T(8,128)S(1)}, u32[]{:S(2)}, u32[]{:S(2)}) collective-permute-start(f32[64,50,1]{0,1,2:T(8,128)S(1)} %copy.80), channel_id=1, source_target_pairs={{0,1},{1,2},{2,3},{4,5},{5,6},{6,7},{8,9},{9,10},{10,11},{12,13},{... | collective-permute-start | bytes 38408 | tf_op jit(solution)/shard_map/ppermute | solution.py:19
  198.7 4.6 %collective-permute-start.12 = (f32[64,50,1]{0,2,1:T(1,128)S(1)}, f32[64,50,1]{0,2,1:T(1,128)S(1)}, u32[]{:S(2)}, u32[]{:S(2)}) collective-permute-start(f32[64,50,1]{0,2,1:T(1,128)S(1)} %get-tuple-element.112), channel_id=1, source_target_pairs={{1,0},{2,1},{3,2},{5,4},{6,5},{7,6},{9,8},{10,9},{11,10},{13,12},{... | collective-permute-start | bytes 38408 | tf_op jit(solution)/shard_map/ppermute | solution.py:20
  203.8 14.9 %copy-start.19 = (pred[64]{0:T(512)(128)(4,1)S(1)}, pred[64]{0:T(512)(128)(4,1)}, u32[]{:S(2)}) copy-start(pred[64]{0:T(512)(128)(4,1)} %get-tuple-element.105) | copy-start | bytes 196
  219.7 3.0 collective-permute-start.13
  303.2 23.2 %copy-start.21 = (pred[352]{0:T(512)(128)(4,1)S(1)}, pred[352]{0:T(512)(128)(4,1)}, u32[]{:S(2)}) copy-start(pred[352]{0:T(512)(128)(4,1)} %compare_and_fusion.4) | copy-start | bytes 1060
  (24 other events, 134.2 us)
Sparse Core Ops, SparseCore 0:
  49.7 82.9 all-gather.4
  224.2 78.9 all-gather.6
where the time goes:
time: 369 us; the launch traced here: 366 us
  waiting for transfers between devices  153 us (41%)
  local copies, waits for them, and re-layouts  107 us (29%)
  other arithmetic  55 us (15%)
  starting transfers between devices  37.3 us (10%)
  between operations  14 us (4%)
    all_gather x2, waiting for transfers between devices, donor_ghosts(): lax.all_gather(crossed[None], ('wide', 'narrow'), axis=0, tiled=True)  135 us
    gather x2, local copies, waits for them, and re-layouts, picker(): received = piece[jnp.clip(donor_row, 0, count - 1), :, donor_entry]  34.9 us
    ppermute x6, starting transfers between devices, extended_2(): before = lax.ppermute(last, axis, up)  25.6 us
    unnamed x69, local copies, waits for them, and re-layouts  13.7 us
    ppermute x6, waiting for transfers between devices, extended_2(): after = lax.ppermute(leading, axis, down)  13.2 us
    all_gather x2, local copies, waits for them, and re-layouts, donor_ghosts(): lax.all_gather(crossed[None], ('wide', 'narrow'), axis=0, tiled=True)  11.4 us
    broadcast_in_dim x1, other arithmetic, shards(): return result[None]  9.81 us
    ppermute x6, starting transfers between devices, extended_2(): after = lax.ppermute(leading, axis, down)  9.81 us
  transfers between devices with their start and end apart: 16, of which 8 were waited for; matrix products, arithmetic and copies ran while one was open for 16% of the time, Pallas kernels for 0%

commit v1 on v0

v1 whole, which is shorter than its diff:
```python
import math

import jax
import jax.numpy as jnp
from jax import lax
from jax.sharding import PartitionSpec as P

TIME_INCREMENT = 0.5
MARGIN = 0.04
HI = lax.Precision.HIGHEST


def shifted_in(shard, axis, dim, forward):
    peers, length = lax.axis_size(axis), shard.shape[dim]
    if forward:
        pairs = [(i, i + 1) for i in range(peers - 1)]
        piece = lax.index_in_dim(shard, length - 1, axis=dim, keepdims=False)
    else:
        pairs = [(i + 1, i) for i in range(peers - 1)]
        piece = lax.index_in_dim(shard, 0, axis=dim, keepdims=False)
    return lax.ppermute(piece, axis, pairs)


def halos(shard):
    west = shifted_in(shard, "wide", 1, True)
    east = shifted_in(shard, "wide", 1, False)
    upper = shifted_in(shard, "narrow", 2, True)
    lower = shifted_in(shard, "narrow", 2, False)
    return west, east, upper, lower


def corner_in(shard):
    wides, narrows = lax.axis_size("wide"), lax.axis_size("narrow")
    pairs = [
        ((w + 1) * narrows + n + 1, w * narrows + n)
        for w in range(wides - 1)
        for n in range(narrows - 1)
    ]
    return lax.ppermute(shard[:, 0, 0], ("wide", "narrow"), pairs)


def neighbours(x, west, east, upper, lower):
    up = jnp.concatenate([upper[:, :, None], x[:, :, :-1]], axis=2)
    down = jnp.concatenate([x[:, :, 1:], lower[:, :, None]], axis=2)
    left = jnp.concatenate([west[:, None, :], x[:, :-1, :]], axis=1)
    right = jnp.concatenate([x[:, 1:, :], east[:, None, :]], axis=1)
    return up, down, left, right


def inverse_metrics(level_values, row_values, total_rows, level_count):
    radius = 0.55 + 0.45 * (level_values + 0.5) / level_count
    angle_span = 0.5 * math.pi + 2.0 * MARGIN
    colatitude = 0.25 * math.pi - MARGIN + (row_values + 0.5) * angle_span / total_rows
    return (1.0 / radius, 1.0 / jnp.sin(colatitude))


def shards(
    heat_scalar,
    polar_flow_speed,
    azimuthal_flow_speed,
    conduction_coefficient,
    interpolant_anchor_position,
    interpolant_factors,
    boundary_source_slot,
):
    current_state = heat_scalar[0]
    level_count, col_count, row_count = current_state.shape
    speed_theta = polar_flow_speed[0].astype(jnp.float32)
    speed_phi = azimuthal_flow_speed[0].astype(jnp.float32)
    k_local = conduction_coefficient[0]
    row_global = lax.axis_index("narrow") * row_count + jnp.arange(row_count, dtype=jnp.int32)
    radius_inv, sine_inv = inverse_metrics(
        jnp.arange(level_count, dtype=jnp.float32),
        row_global.astype(jnp.float32),
        row_count * lax.axis_size("narrow"),
        level_count,
    )
    r3 = radius_inv[:, None, None]
    s3 = sine_inv[None, None, :]

    k_up, k_down, k_left, k_right = neighbours(k_local, *halos(k_local))
    k_up = jnp.maximum(k_up, k_local)
    k_down = jnp.maximum(k_down, k_local)
    k_left = jnp.maximum(k_left, k_local)
    k_right = jnp.maximum(k_right, k_local)
    k_faces = 0.5 * (k_local[1:] + k_local[:-1])

    r2 = radius_inv[:, None]
    coef_up = r2 * (0.5 * speed_theta[:, :, 0] + r2 * k_up[:, :, 0])
    coef_down = r2 * (-0.5 * speed_theta[:, :, -1] + r2 * k_down[:, :, -1])
    sw = sine_inv[None, :]
    coef_left = r2 * sw * (0.5 * speed_phi[:, 0, :] + r2 * sw * k_left[:, 0, :])
    coef_right = r2 * sw * (-0.5 * speed_phi[:, -1, :] + r2 * sw * k_right[:, -1, :])

    cells = interpolant_anchor_position[0, 0, 0]
    weight_a = interpolant_factors[0, 0, 0, 0]
    weight_b = interpolant_factors[0, 0, 0, 1]
    ext_rows = row_count + 1
    base = (cells // row_count) * ext_rows + cells % row_count
    flat = jnp.arange((col_count + 1) * ext_rows, dtype=jnp.int32)[:, None]
    weights = (
        jnp.where(flat == base[None], (1.0 - weight_a) * (1.0 - weight_b), 0.0)
        + jnp.where(flat == base[None] + 1, weight_a * (1.0 - weight_b), 0.0)
        + jnp.where(flat == base[None] + ext_rows, (1.0 - weight_a) * weight_b, 0.0)
        + jnp.where(flat == base[None] + ext_rows + 1, weight_a * weight_b, 0.0)
    )

    sources = boundary_source_slot[0, 0, 0]
    usable = (sources >= 0)[:, None]
    picks = jnp.clip(sources, 0)

    def ghosts_of(x, east, lower, corner):
        xe = jnp.concatenate([x, east[:, None, :]], axis=1)
        lower_e = jnp.concatenate([lower, corner[:, None]], axis=1)
        ext = jnp.concatenate([xe, lower_e[:, :, None]], axis=2)
        ext = ext.reshape(level_count, -1)
        values = jnp.einsum("ke,lk->el", weights, ext, precision=HI)
        crossed = lax.ppermute(values, "panel", [(0, 1), (1, 0)])
        table = lax.all_gather(crossed, ("wide", "narrow"), axis=0, tiled=True)
        got = jnp.take(table, picks, axis=0, mode="clip")
        got = jnp.where(usable, got, 0.0).T
        c = col_count
        return got[:, :c], got[:, c : 2 * c], got[:, 2 * c : 2 * c + row_count], got[:, 2 * c + row_count :]

    def bulk_rate(x, west, east, upper, lower):
        up, down, left, right = neighbours(x, west, east, upper, lower)
        transport = -0.5 * r3 * (speed_theta * (down - up) + speed_phi * s3 * (right - left))
        spread = (
            r3
            * r3
            * (
                k_down * (down - x)
                - k_up * (x - up)
                + s3 * s3 * (k_right * (right - x) - k_left * (x - left))
            )
        )
        fluxes = k_faces * (x[1:] - x[:-1])
        zero = jnp.zeros_like(x[:1])
        radial = jnp.concatenate([fluxes, zero], axis=0) - jnp.concatenate([zero, fluxes], axis=0)
        return transport + spread + radial

    def correction(g_up, g_down, g_left, g_right):
        c_up = coef_up * g_up
        c_down = coef_down * g_down
        c_left = coef_left * g_left
        c_right = coef_right * g_right
        rows = jnp.pad(c_up[:, :, None], ((0, 0), (0, 0), (0, row_count - 1))) + jnp.pad(
            c_down[:, :, None], ((0, 0), (0, 0), (row_count - 1, 0))
        )
        cols = jnp.pad(c_left[:, None, :], ((0, 0), (0, col_count - 1), (0, 0))) + jnp.pad(
            c_right[:, None, :], ((0, 0), (col_count - 1, 0), (0, 0))
        )
        return rows + cols

    def evaluate(x):
        west, east, upper, lower = halos(x)
        corner = corner_in(x)
        ghosts = ghosts_of(x, east, lower, corner)
        bulk = lax.optimization_barrier(bulk_rate(x, west, east, upper, lower))
        return bulk + correction(*ghosts)

    predictor_state = current_state + TIME_INCREMENT * evaluate(current_state)
    result = 0.5 * (
        current_state + predictor_state + TIME_INCREMENT * evaluate(predictor_state)
    )
    return result[None]


def solution(mesh):
    placed = (
        P("panel", None, "wide", "narrow"),
        P("panel", None, "wide", "narrow"),
        P("panel", None, "wide", "narrow"),
        P("panel", None, "wide", "narrow"),
        P("panel", "narrow", "wide", None),
        P("panel", "narrow", "wide", None, None),
        P("panel", "narrow", "wide", None),
    )
    return jax.shard_map(
        shards,
        mesh=mesh,
        in_specs=placed,
        out_specs=P("panel", None, "wide", "narrow"),
        check_vma=False,
    )
```

time: 369 us -> 309 us (0.84)
  waiting for transfers between devices: 153 us -> 95.9 us
  local copies, waits for them, and re-layouts: 107 us -> 84.2 us
  matrix products: 0 us -> 9.57 us
  other arithmetic: 55 us -> 61.7 us
  starting transfers between devices: 37.3 us -> 41.6 us
    all_gather x2, waiting for transfers between devices: 135 us -> 81.8 us  [ghosts_of(): table = lax.all_gather(crossed, ('wide', 'narrow'), axis=0, tiled=True)]
    gather x10 -> x2, local copies, waits for them, and re-layouts: 59.3 us -> 6.56 us  [ghosts_of(): got = jnp.take(table, picks, axis=0, mode='clip')]
    slice x4 -> x8, local copies, waits for them, and re-layouts: 2.21 us -> 29.1 us  [the longest x2 11 us: neighbours(): down = jnp.concatenate([x[:, :, 1:], lower[:, :, None]], axis=2)]
    all_gather x2 -> x0, local copies, waits for them, and re-layouts: 11.4 us -> none  [donor_ghosts(): lax.all_gather(crossed[None], ('wide', 'narrow'), axis=0, tiled=True)]
    unnamed x69 -> x104, local copies, waits for them, and re-layouts: 13.7 us -> 24.3 us
    scatter-add x8 -> x0, local copies, waits for them, and re-layouts: 10.3 us -> none  [the longest x4 6.99 us: with_rim(): return extended.at[:, 0, 1:-1].add(west_rim).at[:, -1, 1:-1].add(east_rim)]
    squeeze x0 -> x10, local copies, waits for them, and re-layouts: none -> 10.2 us  [the longest x1 3.38 us: shards(): current_state = heat_scalar[0]]
    dot_general x0 -> x2, matrix products: none -> 9.57 us  [ghosts_of(): values = jnp.einsum('ke,lk->el', weights, ext, precision=HI)]
  transfers between devices with their start and end apart: 16 -> 18, of which waited for: 8 -> 7; matrix products, arithmetic and copies ran while one was open for 16% -> 35% of each run, Pallas kernels for 0% -> 0%
where the time goes in v1:
time: 309 us; the launch traced here: 307 us
  waiting for transfers between devices  95.9 us (31%)
  local copies, waits for them, and re-layouts  84.2 us (27%)
  other arithmetic  61.7 us (20%)
  starting transfers between devices  41.6 us (13%)
  between operations  14.2 us (5%)
  matrix products  9.57 us (3%)
    all_gather x2, waiting for transfers between devices, ghosts_of(): table = lax.all_gather(crossed, ('wide', 'narrow'), axis=0, tiled=True)  81.8 us
    ppermute x12, starting transfers between devices, shifted_in(): return lax.ppermute(piece, axis, pairs)  38.4 us
    unnamed x104, local copies, waits for them, and re-layouts  24.3 us
    add x2, other arithmetic, bulk_rate(): return transport + spread + radial  19.3 us
    slice x2, local copies, waits for them, and re-layouts, neighbours(): down = jnp.concatenate([x[:, :, 1:], lower[:, :, None]], axis=2)  11 us
    dot_general x2, matrix products, ghosts_of(): values = jnp.einsum('ke,lk->el', weights, ext, precision=HI)  9.57 us
    reshape x2, local copies, waits for them, and re-layouts, ghosts_of(): ext = ext.reshape(level_count, -1)  8.99 us
    sub x1, other arithmetic, bulk_rate(): k_down * (down - x) - k_up * (x - up)  8.05 us
  transfers between devices with their start and end apart: 18, of which 7 were waited for; matrix products, arithmetic and copies ran while one was open for 35% of the time, Pallas kernels for 0%

profile of v1, /device:TPU:1, one launch (start us, length us, event | category | flops | bytes accessed | tf_op | source)
XLA Modules:
  0.0 307.2 jit_solution(3877772666559297289)
XLA Ops:
  10.8 5.2 %collective-permute-start.5 = (f32[64,48]{0,1:T(8,128)}, f32[64,48]{0,1:T(8,128)}, u32[]{:S(2)}, u32[]{:S(2)}) collective-permute-start(f32[64,48]{0,1:T(8,128)} %get-tuple-element.38), channel_id=1, source_target_pairs={{0,1},{1,2},{2,3},{4,5},{5,6},{6,7},{8,9},{9,10},{10,11},{12,13},{... | collective-permute-start | bytes 36872 | tf_op jit(solution)/shard_map/ppermute | solution.py:21
  22.1 4.6 %collective-permute-start.1 = (f32[64,48]{0,1:T(8,128)}, f32[64,48]{0,1:T(8,128)}, u32[]{:S(2)}, u32[]{:S(2)}) collective-permute-start(f32[64,48]{0,1:T(8,128)} %get-tuple-element.45), channel_id=1, source_target_pairs={{0,1},{1,2},{2,3},{4,5},{5,6},{6,7},{8,9},{9,10},{10,11},{12,13},{... | collective-permute-start | bytes 36872 | tf_op jit(solution)/shard_map/ppermute | solution.py:21
  30.4 5.9 %fusion.69 = (f32[64,48,127]{0,1,2:T(8,128)}, f32[64,48,127]{0,1,2:T(8,128)}) fusion(f32[64,48,128]{0,1,2:T(8,128)} %bitcast.217), kind=kLoop, calls=%fused_computation.164 | loop fusion | bytes 6242304 | tf_op jit(solution)/shard_map/slice | solution.py:43
  48.8 3.4 %bitcast_convert_fusion = f32[64,48,128]{0,2,1:T(8,128)} fusion(bf16[1,64,48,128]{1,3,2,0:T(8,128)(2,1)} %copy.82), kind=kLoop, calls=%fused_computation.57 | loop fusion | flops 393216 | bytes 2359296 | tf_op jit(solution)/shard_map/convert_element_type | solution.py:69
  55.9 5.7 %collective-permute-start.6 = (f32[64,128]{0,1:T(8,128)S(1)}, f32[64,128]{0,1:T(8,128)S(1)}, u32[]{:S(2)}, u32[]{:S(2)}) collective-permute-start(f32[64,128]{0,1:T(8,128)S(1)} %bitcast.234), channel_id=1, source_target_pairs={{4,0},{8,4},{12,8},{16,12},{20,16},{24,20},{28,24},{32,28},{36,32}... | collective-permute-start | bytes 98312 | tf_op jit(solution)/shard_map/ppermute | solution.py:21
  63.5 5.1 %collective-permute-done.2 = f32[64,128]{0,1:T(8,128)S(1)} collective-permute-done((f32[64,128]{0,1:T(8,128)S(1)}, f32[64,128]{0,1:T(8,128)S(1)}, u32[]{:S(2)}, u32[]{:S(2)}) %collective-permute-start.2) | collective-permute-done | bytes 32800 | tf_op jit(solution)/shard_map/ppermute | solution.py:21
  70.7 4.5 %reshape.212 = f32[64,6321]{0,1:T(8,128)} reshape(f32[64,49,129]{0,2,1:T(8,128)} %pad_maximum_fusion) | data formatting | bytes 3236352 | tf_op jit(solution)/shard_map/reshape | solution.py:116
  75.2 4.8 %fusion.21 = f32[64,64]{1,0:T(8,128)S(1)} fusion(f32[64,6321]{0,1:T(8,128)} %reshape.212, f32[64]{0:T(128)S(1)} %get-tuple-element.51, s32[64]{0:T(128)S(1)} %get-tuple-element.53, f32[64]{0:T(128)S(1)} %get-tuple-element.49, s32[64]{0:T(128)S(1)} %get-tuple-element.52, f32[64]{0:T(128)S(1)} %get-tuple-element.50, s32[64]{0:T(128)S(1)} %get-tuple-element.5, ...), kind=kOutput, calls=%fused_computation.60 | convolution fusion | flops 315139776 | bytes 1636608 | tf_op jit(solution)/shard_map/ke,lk->el/dot_general | solution.py:117
  96.8 6.1 %fusion.70 = (f32[64,48,127]{0,1,2:T(8,128)}, f32[64,48,127]{0,1,2:T(8,128)}) fusion(f32[64,48,128]{0,1,2:T(8,128)} %copy.78), kind=kLoop, calls=%fused_computation.165 | loop fusion | bytes 6242304 | tf_op jit(solution)/shard_map/slice | solution.py:44
  109.7 3.6 %collective-permute-start.7 = (f32[64,128]{0,1:T(8,128)S(1)}, f32[64,128]{0,1:T(8,128)S(1)}, u32[]{:S(2)}, u32[]{:S(2)}) collective-permute-start(f32[64,128]{0,1:T(8,128)S(1)} %slice_bitcast_fusion.4), channel_id=1, source_target_pairs={{0,4},{4,8},{8,12},{12,16},{16,20},{20,24},{24,28},{28,32},{32,36}... | collective-permute-start | bytes 98312 | tf_op jit(solution)/shard_map/ppermute | solution.py:21
  113.3 8.0 %multiply_subtract_fusion.1 = (f32[64,48,128]{0,1,2:T(8,128)}, f32[64,48,128]{0,1,2:T(8,128)}, f32[64,48,128]{0,1,2:T(8,128)}, f32[64,48,128]{0,1,2:T(8,128)}) fusion(f32[64,48,128]{0,1,2:T(8,128)S(1)} %copy-done.4, f32[64,48,127]{0,1,2:T(8,128)} %get-tuple-element.43, f32[64,48,1]{0,1,2:T(8,128)} %bitcast.8, f32[64,48,1]{0,1,2:T(8,128)S(1)} %bitcast.228, ...), kind=kLoop, calls=%fused_computation.50 | loop fusion | flops 5505024 | bytes 16515072 | tf_op jit(solution)/shard_map/sub | solution.py:132
  125.7 11.8 %fusion.18 = (f32[64,48,128]{0,2,1:T(8,128)}, f32[64,48,128]{0,2,1:T(8,128)}, f32[64,48,128]{0,2,1:T(8,128)}) fusion(f32[64,48,128]{0,1,2:T(8,128)} %get-tuple-element.10, f32[64,48,128]{0,1,2:T(8,128)} %get-tuple-element.15, f32[63,48,128]{0,2,1:T(8,128)} %fusion.2, f32[64,47,128]{0,2,1:T(8,128)} %get-tuple-element.35, f32[64,1,128]{0,2,1:T(8,128)S(1)} %bitcast.231, ...), kind=kLoop, calls=%fused_computation.41 | loop fusion | flops 8257536 | bytes 19637760 | tf_op jit(solution)/shard_map/add | solution.py:140
  137.5 30.1 %all-gather.3.cloned.1.call-done = f32[8192,64]{1,0:T(8,128)} async-done(((f32[64,64]{1,0:T(8,128)}), f32[8192,64]{1,0:T(8,128)}) %all-gather.3.cloned.1.call-update) | async-done | bytes 2097168 | tf_op jit(solution)/shard_map/all_gather | solution.py:119
  173.2 3.5 %fusion.15 = f32[64,48,128]{0,2,1:T(8,128)S(1)} fusion(f32[64,48,128]{0,2,1:T(8,128)} %get-tuple-element.7, f32[64,48,128]{0,1,2:T(8,128)S(1)} %pad_add_fusion.1, f32[64,1,128]{0,2,1:T(8,128)S(1)} %get-tuple-element.19, f32[64,1,128]{0,2,1:T(8,128)S(1)} %get-tuple-element.18, f32[1,64,48,128]{1,3,2,0:T(8,128)S(1)} %copy-done.1), kind=kLoop, calls=%fused_computation.37 | loop fusion | flops 1966080 | bytes 6356992 | tf_op jit(solution)/shard_map/add | solution.py:162
  191.4 4.5 %reshape.213 = f32[64,6321]{0,1:T(8,128)} reshape(f32[64,49,129]{0,2,1:T(8,128)} %pad_maximum_fusion.1) | data formatting | bytes 3236352 | tf_op jit(solution)/shard_map/reshape | solution.py:116
  195.9 4.8 %fusion.20 = f32[64,64]{1,0:T(8,128)S(1)} fusion(f32[64,6321]{0,1:T(8,128)} %reshape.213, f32[64]{0:T(128)S(1)} %copy-done.39, s32[64]{0:T(128)S(1)} %copy-done.48, f32[64]{0:T(128)S(1)} %copy-done.35, s32[64]{0:T(128)S(1)} %copy-done.46, f32[64]{0:T(128)S(1)} %copy-done.37, s32[64]{0:T(128)S(1)} %copy-done.42, f32[64]{0:T(128)S(1)} %copy-done.33, ...), kind=kOutput, calls=%fused_computation.59 | convolution fusion | flops 315139776 | bytes 1636608 | tf_op jit(solution)/shard_map/ke,lk->el/dot_general | solution.py:117
  204.2 4.9 %collective-permute-start.11 = (f32[64,48]{0,1:T(8,128)S(1)}, f32[64,48]{0,1:T(8,128)S(1)}, u32[]{:S(2)}, u32[]{:S(2)}) collective-permute-start(f32[64,48]{0,1:T(8,128)S(1)} %get-tuple-element.31), channel_id=1, source_target_pairs={{0,1},{1,2},{2,3},{4,5},{5,6},{6,7},{8,9},{9,10},{10,11},{12,13},{... | collective-permute-start | bytes 36872 | tf_op jit(solution)/shard_map/ppermute | solution.py:21
  209.1 4.9 %fusion.66 = (f32[64,48,127]{0,1,2:T(8,128)S(1)}, f32[64,48,127]{0,1,2:T(8,128)}) fusion(f32[64,48,128]{0,1,2:T(8,128)} %copy-done.5), kind=kLoop, calls=%fused_computation.161 | loop fusion | bytes 6242304 | tf_op jit(solution)/shard_map/slice | solution.py:44
  215.3 3.9 %fusion.65 = (f32[64,47,128]{0,2,1:T(8,128)}, f32[64,47,128]{0,2,1:T(8,128)}) fusion(f32[64,48,128]{0,2,1:T(8,128)S(1)} %fusion.15), kind=kLoop, calls=%fused_computation.160 | loop fusion | bytes 6160384 | tf_op jit(solution)/shard_map/slice | solution.py:46
  219.2 3.4 %collective-permute-start.13 = (f32[64,128]{0,1:T(8,128)S(1)}, f32[64,128]{0,1:T(8,128)S(1)}, u32[]{:S(2)}, u32[]{:S(2)}) collective-permute-start(f32[64,128]{0,1:T(8,128)S(1)} %get-tuple-element.27), channel_id=1, source_target_pairs={{0,4},{4,8},{8,12},{12,16},{16,20},{20,24},{24,28},{28,32},{32,36}... | collective-permute-start | bytes 98312 | tf_op jit(solution)/shard_map/ppermute | solution.py:21
  222.7 4.4 %subtract_multiply_fusion = (f32[64,48,128]{0,1,2:T(8,128)S(1)}, f32[64,48,128]{0,1,2:T(8,128)S(1)}) fusion(f32[64,48,127]{0,1,2:T(8,128)} %get-tuple-element.29, f32[64,48,1]{0,1,2:T(8,128)S(1)} %bitcast.236, f32[64,48,1]{0,1,2:T(8,128)S(1)} %bitcast.229, f32[64,48,127]{0,1,2:T(8,128)S(1)} %get-tuple-element.28, bf16[1,64,48,128]{1,2,3,0:T(8,128)(2,1)S(1)} %copy-done.12, ...), kind=kLoop, calls=%fused_computation.47 | loop fusion | flops 3932160 | bytes 11796480 | tf_op jit(solution)/shard_map/mul | solution.py:127
  227.1 7.5 %fusion.11 = f32[64,48,128]{0,2,1:T(8,128)} fusion(f32[64,48,128]{0,1,2:T(8,128)S(1)} %get-tuple-element.14, f32[64,48,128]{0,1,2:T(8,128)S(1)} %get-tuple-element.13, f32[63,48,128]{0,2,1:T(8,128)S(1)} %fusion, f32[64,48,128]{0,2,1:T(8,128)S(1)} %copy-done.17, f32[64,48,128]{0,2,1:T(8,128)S(1)} %fusion.15, f32[64,48,128]{0,2,1:T(8,128)S(1)} %copy-done.16, ...), kind=kLoop, calls=%fused_computation.31 | loop fusion | flops 7471104 | bytes 14919168 | tf_op jit(solution)/shard_map/add | solution.py:140
  234.7 51.7 %all-gather.5.cloned.1.call-done = f32[8192,64]{1,0:T(8,128)} async-done(((f32[64,64]{1,0:T(8,128)}), f32[8192,64]{1,0:T(8,128)}) %all-gather.5.cloned.1.call-update) | async-done | bytes 2097168 | tf_op jit(solution)/shard_map/all_gather | solution.py:119
  291.7 5.5 %fusion.8 = f32[1,64,48,128]{1,3,2,0:T(8,128)} fusion(f32[64,48,128]{0,2,1:T(8,128)} %fusion.11, f32[64,48,1]{0,2,1:T(1,128)S(1)} %bitcast.227, f32[64,1,128]{0,2,1:T(8,128)S(1)} %get-tuple-element.17, f32[64,1,128]{0,2,1:T(8,128)S(1)} %get-tuple-element.16, f32[64,48,1]{0,2,1:T(1,128)S(1)} %bitcast.226, f32[64,48,128]{0,2,1:T(8,128)S(1)} %fusion.15, ...), kind=kLoop, calls=%fused_computation.27 | loop fusion | flops 3145728 | bytes 6381568 | tf_op jit(solution)/shard_map/broadcast_in_dim | solution.py:166
  (179 shorter events, 95.2 us)
Async XLA Ops:
  6.5 161.0 %all-gather.3.cloned.1.call-start = ((), (), s32[]{:S(2)}) async-start(), calls=%async_computation | async-start | bytes 4227072 | tf_op jit(solution)/shard_map/all_gather | solution.py:119
  9.6 100.1 %collective-permute-start.4 = (f32[64,48]{0,1:T(8,128)}, f32[64,48]{0,1:T(8,128)S(1)}, u32[]{:S(2)}, u32[]{:S(2)}) collective-permute-start(f32[64,48]{0,1:T(8,128)} %get-tuple-element.39), channel_id=1, source_target_pairs={{1,0},{2,1},{3,2},{5,4},{6,5},{7,6},{9,8},{10,9},{11,10},{13,12},{... | collective-permute-start | bytes 36872 | tf_op jit(solution)/shard_map/ppermute | solution.py:21
  10.8 102.4 %collective-permute-start.5 = (f32[64,48]{0,1:T(8,128)}, f32[64,48]{0,1:T(8,128)}, u32[]{:S(2)}, u32[]{:S(2)}) collective-permute-start(f32[64,48]{0,1:T(8,128)} %get-tuple-element.38), channel_id=1, source_target_pairs={{0,1},{1,2},{2,3},{4,5},{5,6},{6,7},{8,9},{9,10},{10,11},{12,13},{... | collective-permute-start | bytes 36872 | tf_op jit(solution)/shard_map/ppermute | solution.py:21
  20.8 40.8 %collective-permute-start = (f32[64,48]{0,1:T(8,128)S(1)}, f32[64,48]{0,1:T(8,128)S(1)}, u32[]{:S(2)}, u32[]{:S(2)}) collective-permute-start(f32[64,48]{0,1:T(8,128)S(1)} %get-tuple-element.44), channel_id=1, source_target_pairs={{1,0},{2,1},{3,2},{5,4},{6,5},{7,6},{9,8},{10,9},{11,10},{13,12},{... | collective-permute-start | bytes 36872 | tf_op jit(solution)/shard_map/ppermute | solution.py:21
  22.1 91.2 %collective-permute-start.1 = (f32[64,48]{0,1:T(8,128)}, f32[64,48]{0,1:T(8,128)}, u32[]{:S(2)}, u32[]{:S(2)}) collective-permute-start(f32[64,48]{0,1:T(8,128)} %get-tuple-element.45), channel_id=1, source_target_pairs={{0,1},{1,2},{2,3},{4,5},{5,6},{6,7},{8,9},{9,10},{10,11},{12,13},{... | collective-permute-start | bytes 36872 | tf_op jit(solution)/shard_map/ppermute | solution.py:21
  28.8 95.0 %copy-start = (f32[1,64,48,128]{1,3,2,0:T(8,128)}, f32[1,64,48,128]{1,3,2,0:T(8,128)S(1)}, u32[]{:S(2)}) copy-start(f32[1,64,48,128]{1,3,2,0:T(8,128)S(1)} %copy.76) | copy-start | bytes 4718596
  28.8 27.1 %collective-permute-start.8 = (f32[64]{0:T(128)S(1)}, f32[64]{0:T(128)S(1)}, u32[]{:S(2)}, u32[]{:S(2)}) collective-permute-start(f32[64]{0:T(128)S(1)} %slice_bitcast_fusion.16), channel_id=1, source_target_pairs={{5,0},{6,1},{7,2},{9,4},{10,5},{11,6},{13,8},{14,9},{15,10},{17,12... | collective-permute-start | bytes 776 | tf_op jit(solution)/shard_map/ppermute | solution.py:39
  48.1 27.0 %copy-start.41 = (s32[64]{0:T(128)}, s32[64]{0:T(128)S(1)}, u32[]{:S(2)}) copy-start(s32[64]{0:T(128)S(1)} %get-tuple-element.5) | copy-start | bytes 772
  48.1 27.0 %copy-start.43 = (s32[64]{0:T(128)}, s32[64]{0:T(128)S(1)}, u32[]{:S(2)}) copy-start(s32[64]{0:T(128)S(1)} %get-tuple-element.6) | copy-start | bytes 772
  48.2 27.0 %copy-start.45 = (s32[64]{0:T(128)}, s32[64]{0:T(128)S(1)}, u32[]{:S(2)}) copy-start(s32[64]{0:T(128)S(1)} %get-tuple-element.52) | copy-start | bytes 772
  55.9 65.5 %collective-permute-start.6 = (f32[64,128]{0,1:T(8,128)S(1)}, f32[64,128]{0,1:T(8,128)S(1)}, u32[]{:S(2)}, u32[]{:S(2)}) collective-permute-start(f32[64,128]{0,1:T(8,128)S(1)} %bitcast.234), channel_id=1, source_target_pairs={{4,0},{8,4},{12,8},{16,12},{20,16},{24,20},{28,24},{32,28},{36,32}... | collective-permute-start | bytes 98312 | tf_op jit(solution)/shard_map/ppermute | solution.py:21
  61.6 7.1 %collective-permute-start.2 = (f32[64,128]{0,1:T(8,128)S(1)}, f32[64,128]{0,1:T(8,128)S(1)}, u32[]{:S(2)}, u32[]{:S(2)}) collective-permute-start(f32[64,128]{0,1:T(8,128)S(1)} %get-tuple-element.36), channel_id=1, source_target_pairs={{4,0},{8,4},{12,8},{16,12},{20,16},{24,20},{28,24},{32,28},{36,32}... | collective-permute-start | bytes 98312 | tf_op jit(solution)/shard_map/ppermute | solution.py:21
  80.0 2.9 collective-permute-start.9
  82.9 40.9 %collective-permute-start.3 = (f32[64,128]{0,1:T(8,128)}, f32[64,128]{0,1:T(8,128)S(1)}, u32[]{:S(2)}, u32[]{:S(2)}) collective-permute-start(f32[64,128]{0,1:T(8,128)} %get-tuple-element.37), channel_id=1, source_target_pairs={{0,4},{4,8},{8,12},{12,16},{16,20},{20,24},{24,28},{28,32},{32,36}... | collective-permute-start | bytes 98312 | tf_op jit(solution)/shard_map/ppermute | solution.py:21
  85.8 200.6 %all-gather.5.cloned.1.call-start = ((), (), s32[]{:S(2)}) async-start(), calls=%async_computation.1 | async-start | bytes 4227072 | tf_op jit(solution)/shard_map/all_gather | solution.py:119
  109.7 12.0 %collective-permute-start.7 = (f32[64,128]{0,1:T(8,128)S(1)}, f32[64,128]{0,1:T(8,128)S(1)}, u32[]{:S(2)}, u32[]{:S(2)}) collective-permute-start(f32[64,128]{0,1:T(8,128)S(1)} %slice_bitcast_fusion.4), channel_id=1, source_target_pairs={{0,4},{4,8},{8,12},{12,16},{16,20},{20,24},{24,28},{28,32},{32,36}... | collective-permute-start | bytes 98312 | tf_op jit(solution)/shard_map/ppermute | solution.py:21
  125.7 41.9 %copy-start.25 = (s32[1024]{0:T(1024)S(1)}, s32[1024]{0:T(1024)}, u32[]{:S(2)}) copy-start(s32[1024]{0:T(1024)} %pad_clamp_fusion) | copy-start | bytes 12292
  125.7 45.2 %copy-start.28 = (pred[352]{0:T(512)(128)(4,1)S(1)}, pred[352]{0:T(512)(128)(4,1)}, u32[]{:S(2)}) copy-start(pred[352]{0:T(512)(128)(4,1)} %compare_reduce_fusion) | copy-start | bytes 1060
  180.2 8.0 %collective-permute-start.10 = (f32[64,48]{0,1:T(8,128)S(1)}, f32[64,48]{0,1:T(8,128)S(1)}, u32[]{:S(2)}, u32[]{:S(2)}) collective-permute-start(f32[64,48]{0,1:T(8,128)S(1)} %get-tuple-element.30), channel_id=1, source_target_pairs={{1,0},{2,1},{3,2},{5,4},{6,5},{7,6},{9,8},{10,9},{11,10},{13,12},{... | collective-permute-start | bytes 36872 | tf_op jit(solution)/shard_map/ppermute | solution.py:21
  181.5 6.7 %collective-permute-start.14 = (f32[64]{0:T(128)S(1)}, f32[64]{0:T(128)S(1)}, u32[]{:S(2)}, u32[]{:S(2)}) collective-permute-start(f32[64]{0:T(128)S(1)} %slice_bitcast_fusion.15), channel_id=1, source_target_pairs={{5,0},{6,1},{7,2},{9,4},{10,5},{11,6},{13,8},{14,9},{15,10},{17,12... | collective-permute-start | bytes 776 | tf_op jit(solution)/shard_map/ppermute | solution.py:39
  182.8 6.5 %collective-permute-start.12 = (f32[64,128]{0,1:T(8,128)S(1)}, f32[64,128]{0,1:T(8,128)S(1)}, u32[]{:S(2)}, u32[]{:S(2)}) collective-permute-start(f32[64,128]{0,1:T(8,128)S(1)} %get-tuple-element.26), channel_id=1, source_target_pairs={{4,0},{8,4},{12,8},{16,12},{20,16},{24,20},{28,24},{32,28},{36,32}... | collective-permute-start | bytes 98312 | tf_op jit(solution)/shard_map/ppermute | solution.py:21
  200.7 2.9 collective-permute-start.15
  204.2 18.4 %collective-permute-start.11 = (f32[64,48]{0,1:T(8,128)S(1)}, f32[64,48]{0,1:T(8,128)S(1)}, u32[]{:S(2)}, u32[]{:S(2)}) collective-permute-start(f32[64,48]{0,1:T(8,128)S(1)} %get-tuple-element.31), channel_id=1, source_target_pairs={{0,1},{1,2},{2,3},{4,5},{5,6},{6,7},{8,9},{9,10},{10,11},{12,13},{... | collective-permute-start | bytes 36872 | tf_op jit(solution)/shard_map/ppermute | solution.py:21
  219.2 7.9 %collective-permute-start.13 = (f32[64,128]{0,1:T(8,128)S(1)}, f32[64,128]{0,1:T(8,128)S(1)}, u32[]{:S(2)}, u32[]{:S(2)}) collective-permute-start(f32[64,128]{0,1:T(8,128)S(1)} %get-tuple-element.27), channel_id=1, source_target_pairs={{0,4},{4,8},{8,12},{12,16},{16,20},{20,24},{24,28},{28,32},{32,36}... | collective-permute-start | bytes 98312 | tf_op jit(solution)/shard_map/ppermute | solution.py:21
  (43 other events, 320.1 us)
Sparse Core Ops, SparseCore 0:
  85.9 81.6 all-gather.2
  204.3 82.0 all-gather.4

commit v2 on v1

--- a/solution.py
+++ b/solution.py
@@ -95,28 +95,50 @@
     cells = interpolant_anchor_position[0, 0, 0]
     weight_a = interpolant_factors[0, 0, 0, 0]
     weight_b = interpolant_factors[0, 0, 0, 1]
-    ext_rows = row_count + 1
-    base = (cells // row_count) * ext_rows + cells % row_count
-    flat = jnp.arange((col_count + 1) * ext_rows, dtype=jnp.int32)[:, None]
-    weights = (
-        jnp.where(flat == base[None], (1.0 - weight_a) * (1.0 - weight_b), 0.0)
-        + jnp.where(flat == base[None] + 1, weight_a * (1.0 - weight_b), 0.0)
-        + jnp.where(flat == base[None] + ext_rows, (1.0 - weight_a) * weight_b, 0.0)
-        + jnp.where(flat == base[None] + ext_rows + 1, weight_a * weight_b, 0.0)
+    col0 = (cells // row_count)[None]
+    row0 = (cells % row_count)[None]
+    rows_at = jnp.arange(row_count + 1, dtype=jnp.int32)[:, None]
+    cols_at = jnp.arange(col_count + 1, dtype=jnp.int32)[:, None]
+    w_rows = jnp.where(rows_at == row0, 1.0 - weight_a, 0.0) + jnp.where(
+        rows_at == row0 + 1, weight_a, 0.0
+    )
+    w_cols = jnp.where(cols_at == col0, 1.0 - weight_b, 0.0) + jnp.where(
+        cols_at == col0 + 1, weight_b, 0.0
     )
 
     sources = boundary_source_slot[0, 0, 0]
     usable = (sources >= 0)[:, None]
-    picks = jnp.clip(sources, 0)
+    capacity = cells.shape[0]
+    narrows = lax.axis_size("narrow")
+    donor_tile = jnp.clip(sources, 0) // capacity
+    t_w = (donor_tile // narrows) ^ lax.axis_index("wide")
+    t_n = (donor_tile % narrows) ^ lax.axis_index("narrow")
+    position = ((t_w >> 1) & 3) + 4 * (t_n & 3) + 16 * ((t_w >> 3) & 3) + 64 * (t_w & 1)
+    picks = position * capacity + jnp.clip(sources, 0) % capacity
+
+    def gathered(values):
+        wides = lax.axis_size("wide")
+        parts = []
+        for o in range(4):
+            pairs = [(p * wides + w, (1 - p) * wides + (w ^ (o << 1))) for p in range(2) for w in range(wides)]
+            parts.append(lax.ppermute(values, ("panel", "wide"), pairs))
+        values = jnp.concatenate(parts, axis=0)
+        for axis, shift, bits in (("narrow", 0, 2), ("wide", 3, 2), ("wide", 0, 1)):
+            n = lax.axis_size(axis)
+            parts = [values]
+            for o in range(1, 1 << bits):
+                parts.append(lax.ppermute(values, axis, [(i, i ^ (o << shift)) for i in range(n)]))
+            values = jnp.concatenate(parts, axis=0)
+        return values
 
     def ghosts_of(x, east, lower, corner):
-        xe = jnp.concatenate([x, east[:, None, :]], axis=1)
-        lower_e = jnp.concatenate([lower, corner[:, None]], axis=1)
-        ext = jnp.concatenate([xe, lower_e[:, :, None]], axis=2)
-        ext = ext.reshape(level_count, -1)
-        values = jnp.einsum("ke,lk->el", weights, ext, precision=HI)
-        crossed = lax.ppermute(values, "panel", [(0, 1), (1, 0)])
-        table = lax.all_gather(crossed, ("wide", "narrow"), axis=0, tiled=True)
+        lc = level_count
+        partial = jnp.dot(x.reshape(lc * col_count, row_count), w_rows[:row_count], precision=HI)
+        values = jnp.sum(partial.reshape(lc, col_count, capacity) * w_cols[None, :col_count], axis=1)
+        values = values + jnp.dot(east, w_rows[:row_count], precision=HI) * w_cols[col_count]
+        values = values + jnp.dot(lower, w_cols[:col_count], precision=HI) * w_rows[row_count]
+        values = values + corner[:, None] * (w_cols[col_count] * w_rows[row_count])[None]
+        table = gathered(values.T)
         got = jnp.take(table, picks, axis=0, mode="clip")
         got = jnp.where(usable, got, 0.0).T
         c = col_count

time: 309 us -> 451 us (1.46); the launches traced: 307 us -> 443 us
  local copies, waits for them, and re-layouts: 84.2 us -> 218 us
  waiting for transfers between devices: 95.9 us -> 44.1 us
  starting transfers between devices: 41.6 us -> 78.7 us
  other arithmetic: 61.7 us -> 96.2 us
  between operations: 14.2 us -> 0.8 us
  matrix products: 9.57 us -> 4.85 us
    all_gather x2 -> x0, waiting for transfers between devices: 81.8 us -> none  [ghosts_of(): table = lax.all_gather(crossed, ('wide', 'narrow'), axis=0, tiled=True)]
    ppermute x2 -> x22, starting transfers between devices: 0.19 us -> 44.2 us  [the longest x14 25.9 us: gathered(): lax.ppermute(values, axis, [(i, i ^ o << shift) for i in range(n)])]
    ppermute x2 -> x22, waiting for transfers between devices: 4.93 us -> 32.5 us  [the longest x14 28.1 us: gathered(): lax.ppermute(values, axis, [(i, i ^ o << shift) for i in range(n)])]
    slice x1 -> x9, local copies, waits for them, and re-layouts: 1.79 us -> 28.6 us  [the longest x3 16.4 us: shifted_in(): piece = lax.index_in_dim(shard, length - 1, axis=dim, keepdims=False)]
    broadcast_in_dim x3 -> x8, local copies, waits for them, and re-layouts: 3.25 us -> 29.7 us  [the longest x3 13.4 us: neighbours(): left = jnp.concatenate([west[:, None, :], x[:, :-1, :]], axis=1)]
    mul x4, other arithmetic: 5.25 us -> 27.7 us  [the longest x1 22.6 us: bulk_rate(): r3 * r3]
    slice x1 -> x5, local copies, waits for them, and re-layouts: 1.08 us -> 18.9 us  [shifted_in(): piece = lax.index_in_dim(shard, 0, axis=dim, keepdims=False)]
    add x2 -> x3, other arithmetic: 19.3 us -> 36.4 us  [bulk_rate(): return transport + spread + radial]
  transfers between devices with their start and end apart: 18 -> 36, of which waited for: 7 -> 11; matrix products, arithmetic and copies ran while one was open for 35% -> 57% of each run, Pallas kernels for 0% -> 0%
where the time goes in v2:
time: 451 us; the launch traced here: 443 us
  local copies, waits for them, and re-layouts  218 us (48%)
  other arithmetic  96.2 us (21%)
  starting transfers between devices  78.7 us (17%)
  waiting for transfers between devices  44.1 us (10%)
  matrix products  4.85 us (1%)
    add x3, other arithmetic, bulk_rate(): return transport + spread + radial  36.4 us
    unnamed x72, local copies, waits for them, and re-layouts  35.8 us
    ppermute x12, starting transfers between devices, shifted_in(): return lax.ppermute(piece, axis, pairs)  32 us
    ppermute x14, waiting for transfers between devices, gathered(): lax.ppermute(values, axis, [(i, i ^ o << shift) for i in range(n)])  28.1 us
    ppermute x14, starting transfers between devices, gathered(): lax.ppermute(values, axis, [(i, i ^ o << shift) for i in range(n)])  25.9 us
    mul x1, other arithmetic, bulk_rate(): r3 * r3  22.6 us
    slice x5, local copies, waits for them, and re-layouts, shifted_in(): piece = lax.index_in_dim(shard, 0, axis=dim, keepdims=False)  18.9 us
    ppermute x8, starting transfers between devices, gathered(): parts.append(lax.ppermute(values, ('panel', 'wide'), pairs))  18.2 us
  transfers between devices with their start and end apart: 36, of which 11 were waited for; matrix products, arithmetic and copies ran while one was open for 57% of the time, Pallas kernels for 0%

profile of v2, /device:TPU:1, one launch (start us, length us, event | category | flops | bytes accessed | tf_op | source)
XLA Modules:
  0.0 442.6 jit_solution(16633907394497951007)
XLA Ops:
  0.0 5.5 %copy.677 = f32[1,64,48,128]{2,1,3,0:T(8,128)} copy(f32[1,64,48,128]{3,2,1,0:T(8,128)} %param.7) | data formatting | bytes 3145728 | tf_op args[0]
  5.5 8.0 %fusion.55 = (f32[64,1,128]{1,0,2:T(8,128)}, f32[64,1,128]{1,0,2:T(8,128)}) fusion(f32[64,48,128]{1,0,2:T(8,128)} %bitcast.210), kind=kLoop, calls=%fused_computation.214 | loop fusion | bytes 131072 | tf_op jit(solution)/shard_map/slice | solution.py:20
  17.4 6.3 %collective-permute-start.3 = (f32[64,128]{1,0:T(8,128)S(1)}, f32[64,128]{1,0:T(8,128)S(1)}, u32[]{:S(2)}, u32[]{:S(2)}) collective-permute-start(f32[64,128]{1,0:T(8,128)S(1)} %bitcast.233), channel_id=1, source_target_pairs={{0,4},{4,8},{8,12},{12,16},{16,20},{20,24},{24,28},{28,32},{32,36}... | collective-permute-start | bytes 98312 | tf_op jit(solution)/shard_map/ppermute | solution.py:21
  32.6 4.5 %copy.685 = f32[1,64,48,128]{2,1,3,0:T(8,128)} copy(f32[1,64,48,128]{3,2,1,0:T(8,128)S(1)} %copy-done.3) | data formatting | bytes 3145728 | tf_op args[3]
  37.1 8.2 %fusion.50 = (f32[64,1,128]{1,0,2:T(8,128)}, f32[64,1,128]{1,0,2:T(8,128)}) fusion(f32[64,48,128]{1,0,2:T(8,128)} %bitcast.215), kind=kLoop, calls=%fused_computation.209 | loop fusion | bytes 131072 | tf_op jit(solution)/shard_map/slice | solution.py:17
  55.9 5.0 %collective-permute-start.7 = (f32[64,128]{1,0:T(8,128)}, f32[64,128]{1,0:T(8,128)S(1)}, u32[]{:S(2)}, u32[]{:S(2)}) collective-permute-start(f32[64,128]{1,0:T(8,128)} %bitcast.19), channel_id=1, source_target_pairs={{0,4},{4,8},{8,12},{12,16},{16,20},{20,24},{24,28},{28,32},{32,36}... | collective-permute-start | bytes 98312 | tf_op jit(solution)/shard_map/ppermute | solution.py:21
  60.9 8.1 %fusion.54 = (f32[64,47,128]{1,0,2:T(8,128)}, f32[64,47,128]{1,0,2:T(8,128)}) fusion(f32[64,48,128]{1,0,2:T(8,128)} %bitcast.212), kind=kLoop, calls=%fused_computation.213 | loop fusion | bytes 6160384 | tf_op jit(solution)/shard_map/slice | solution.py:46
  78.4 4.6 %fusion.51 = (f32[64,47,128]{1,0,2:T(8,128)}, f32[64,47,128]{1,0,2:T(8,128)}) fusion(f32[64,48,128]{1,0,2:T(8,128)S(1)} %bitcast.218), kind=kLoop, calls=%fused_computation.210 | loop fusion | bytes 6160384 | tf_op jit(solution)/shard_map/slice | solution.py:45
  84.5 4.7 %copy.679 = bf16[1,64,48,128]{2,1,3,0:T(8,128)(2,1)} copy(bf16[1,64,48,128]{3,2,1,0:T(8,128)(2,1)} %param.9) | data formatting | bytes 1572864 | tf_op args[2]
  89.2 4.6 %copy.678 = bf16[1,64,48,128]{2,1,3,0:T(8,128)(2,1)} copy(bf16[1,64,48,128]{3,2,1,0:T(8,128)(2,1)} %param.8) | data formatting | bytes 1572864 | tf_op args[1]
  103.3 4.8 %slice_multiply_fusion = (f32[64,1,128]{1,0,2:T(8,128)}, f32[64,1,128]{1,0,2:T(8,128)}) fusion(f32[64,48,128]{1,0,2:T(8,128)S(1)} %bitcast_convert_fusion), kind=kLoop, calls=%fused_computation.2 | loop fusion | flops 16384 | bytes 131072 | tf_op jit(solution)/shard_map/mul | solution.py:93
  110.9 5.4 %collective-permute-done.8 = f32[64]{0:T(128)S(1)} collective-permute-done((f32[64]{0:T(128)S(1)}, f32[64]{0:T(128)S(1)}, u32[]{:S(2)}, u32[]{:S(2)}) %collective-permute-start.8) | collective-permute-done | bytes 288 | tf_op jit(solution)/shard_map/ppermute | solution.py:39
  118.6 6.6 %collective-permute-start.10 = (f32[64,64]{1,0:T(8,128)S(1)}, f32[64,64]{1,0:T(8,128)S(1)}, u32[]{:S(2)}, u32[]{:S(2)}) collective-permute-start(f32[64,64]{1,0:T(8,128)S(1)} %fusion.14), channel_id=1, source_target_pairs={{0,136},{4,140},{8,128},{12,132},{16,152},{20,156},{24,144},{28,14... | collective-permute-start | bytes 49160 | tf_op jit(solution)/shard_map/ppermute | solution.py:124
  186.8 10.6 %collective-permute-done.18 = f32[1024,64]{1,0:T(8,128)S(1)} collective-permute-done((f32[1024,64]{1,0:T(8,128)}, f32[1024,64]{1,0:T(8,128)S(1)}, u32[]{:S(2)}, u32[]{:S(2)}) %collective-permute-start.18) | collective-permute-done | bytes 262176 | tf_op jit(solution)/shard_map/ppermute | solution.py:130
  204.6 29.5 %multiply_add_fusion.1 = (f32[64,48,128]{1,0,2:T(8,128)}, f32[64,48,128]{1,0,2:T(8,128)}, f32[64,48,128]{1,0,2:T(8,128)}, f32[64,48,128]{1,0,2:T(8,128)}, f32[64,48,128]{1,0,2:T(8,128)}) fusion(f32[64,47,128]{1,0,2:T(8,128)} %get-tuple-element.42, f32[64,1,128]{1,0,2:T(8,128)} %copy.683, f32[64,1,128]{1,0,2:T(8,128)} %copy.681, ...), kind=kLoop, calls=%fused_computation.19 | loop fusion | flops 13762560 | bytes 25167360 | tf_op jit(solution)/shard_map/add | solution.py:162
  265.3 4.7 %copy.702 = f32[64,48,128]{2,1,0:T(8,128)} copy(f32[64,48,128]{1,0,2:T(8,128)} %pad_add_fusion) | data formatting | bytes 3145728 | tf_op jit(solution)/shard_map/add | solution.py:169
  272.3 4.7 %copy.704 = f32[64,48,128]{1,0,2:T(8,128)} copy(f32[64,48,128]{2,1,0:T(8,128)S(1)} %fusion.3) | data formatting | bytes 3145728 | tf_op jit(solution)/shard_map/add | solution.py:184
  282.7 8.1 %fusion.48 = (f32[64,47,128]{1,0,2:T(8,128)}, f32[64,47,128]{1,0,2:T(8,128)}) fusion(f32[64,48,128]{1,0,2:T(8,128)} %copy.704), kind=kLoop, calls=%fused_computation.207 | loop fusion | bytes 6160384 | tf_op jit(solution)/shard_map/slice | solution.py:46
  294.9 6.1 %collective-permute-done.24 = f32[64]{0:T(128)S(1)} collective-permute-done((f32[64]{0:T(128)S(1)}, f32[64]{0:T(128)S(1)}, u32[]{:S(2)}, u32[]{:S(2)}) %collective-permute-start.24) | collective-permute-done | bytes 288 | tf_op jit(solution)/shard_map/ppermute | solution.py:39
  303.3 8.5 %fusion.49 = (f32[64,48,127]{1,0,2:T(8,128)}, f32[64,48,127]{1,0,2:T(8,128)}) fusion(f32[64,48,128]{1,0,2:T(8,128)} %copy.704), kind=kLoop, calls=%fused_computation.208 | loop fusion | bytes 6242304 | tf_op jit(solution)/shard_map/slice | solution.py:44
  352.6 22.6 %add_multiply_fusion = (f32[64,48,128]{1,0,2:T(8,128)}, f32[64,48,128]{1,0,2:T(8,128)}) fusion(f32[64,48,128]{1,0,2:T(8,128)} %get-tuple-element.16, f32[64,48,128]{1,0,2:T(8,128)} %copy.704, f32[64,48,128]{1,0,2:T(8,128)} %get-tuple-element.15, f32[64,48,128]{1,0,2:T(8,128)} %get-tuple-element.14, f32[64,48,128]{1,0,2:T(8,128)} %get-tuple-element.13, ...), kind=kLoop, calls=%fused_computation.16 | loop fusion | flops 7077888 | bytes 18875136 | tf_op jit(solution)/shard_map/mul | solution.py:151
  375.2 4.7 %copy.730 = f32[64,48,128]{2,1,0:T(8,128)} copy(f32[64,48,128]{1,0,2:T(8,128)} %get-tuple-element.22) | data formatting | bytes 3145728 | tf_op jit(solution)/shard_map/add | solution.py:186
  387.5 9.2 %collective-permute-done.34 = f32[1024,64]{1,0:T(8,128)S(1)} collective-permute-done((f32[1024,64]{1,0:T(8,128)}, f32[1024,64]{1,0:T(8,128)S(1)}, u32[]{:S(2)}, u32[]{:S(2)}) %collective-permute-start.34) | collective-permute-done | bytes 262176 | tf_op jit(solution)/shard_map/ppermute | solution.py:130
  403.9 13.5 %multiply_add_fusion = f32[64,48,128]{1,0,2:T(8,128)} fusion(f32[64,48,127]{1,0,2:T(8,128)} %get-tuple-element.26, f32[64,48,1]{1,0,2:T(8,128)S(1)} %bitcast.226, f32[64,48,1]{1,0,2:T(8,128)S(1)} %bitcast.224, f32[64,48,127]{1,0,2:T(8,128)} %get-tuple-element.25, bf16[1,64,48,128]{2,1,3,0:T(8,128)(2,1)} %copy.679, bf16[1,64,48,128]{2,1,3,0:T(8,128)(2,1)} %copy.678, ...), kind=kLoop, calls=%fused_computation.17 | loop fusion | flops 4718592 | bytes 9437696 | tf_op jit(solution)/shard_map/add | solution.py:149
  (214 shorter events, 243.2 us)
Async XLA Ops:
  17.4 141.0 %collective-permute-start.3 = (f32[64,128]{1,0:T(8,128)S(1)}, f32[64,128]{1,0:T(8,128)S(1)}, u32[]{:S(2)}, u32[]{:S(2)}) collective-permute-start(f32[64,128]{1,0:T(8,128)S(1)} %bitcast.233), channel_id=1, source_target_pairs={{0,4},{4,8},{8,12},{12,16},{16,20},{20,24},{24,28},{28,32},{32,36}... | collective-permute-start | bytes 98312 | tf_op jit(solution)/shard_map/ppermute | solution.py:21
  28.0 88.3 %collective-permute-start.2 = (f32[64,128]{1,0:T(8,128)}, f32[64,128]{1,0:T(8,128)S(1)}, u32[]{:S(2)}, u32[]{:S(2)}) collective-permute-start(f32[64,128]{1,0:T(8,128)} %bitcast.8), channel_id=1, source_target_pairs={{4,0},{8,4},{12,8},{16,12},{20,16},{24,20},{28,24},{32,28},{36,32}... | collective-permute-start | bytes 98312 | tf_op jit(solution)/shard_map/ppermute | solution.py:21
  31.3 78.1 %collective-permute-start = (f32[64,48]{1,0:T(8,128)}, f32[64,48]{1,0:T(8,128)S(1)}, u32[]{:S(2)}, u32[]{:S(2)}) collective-permute-start(f32[64,48]{1,0:T(8,128)} %get-tuple-element.39), channel_id=1, source_target_pairs={{1,0},{2,1},{3,2},{5,4},{6,5},{7,6},{9,8},{10,9},{11,10},{13,12},{... | collective-permute-start | bytes 36872 | tf_op jit(solution)/shard_map/ppermute | solution.py:21
  49.7 120.6 %collective-permute-start.6 = (f32[64,128]{1,0:T(8,128)}, f32[64,128]{1,0:T(8,128)S(1)}, u32[]{:S(2)}, u32[]{:S(2)}) collective-permute-start(f32[64,128]{1,0:T(8,128)} %bitcast.17), channel_id=1, source_target_pairs={{4,0},{8,4},{12,8},{16,12},{20,16},{24,20},{28,24},{32,28},{36,32}... | collective-permute-start | bytes 98312 | tf_op jit(solution)/shard_map/ppermute | solution.py:21
  55.9 120.1 %collective-permute-start.7 = (f32[64,128]{1,0:T(8,128)}, f32[64,128]{1,0:T(8,128)S(1)}, u32[]{:S(2)}, u32[]{:S(2)}) collective-permute-start(f32[64,128]{1,0:T(8,128)} %bitcast.19), channel_id=1, source_target_pairs={{0,4},{4,8},{8,12},{12,16},{16,20},{20,24},{24,28},{28,32},{32,36}... | collective-permute-start | bytes 98312 | tf_op jit(solution)/shard_map/ppermute | solution.py:21
  116.5 8.7 %collective-permute-start.9 = (f32[64,64]{1,0:T(8,128)S(1)}, f32[64,64]{1,0:T(8,128)S(1)}, u32[]{:S(2)}, u32[]{:S(2)}) collective-permute-start(f32[64,64]{1,0:T(8,128)S(1)} %fusion.14), channel_id=1, source_target_pairs={{0,128},{4,132},{8,136},{12,140},{16,144},{20,148},{24,152},{28,15... | collective-permute-start | bytes 49160 | tf_op jit(solution)/shard_map/ppermute | solution.py:124
  118.6 8.8 %collective-permute-start.10 = (f32[64,64]{1,0:T(8,128)S(1)}, f32[64,64]{1,0:T(8,128)S(1)}, u32[]{:S(2)}, u32[]{:S(2)}) collective-permute-start(f32[64,64]{1,0:T(8,128)S(1)} %fusion.14), channel_id=1, source_target_pairs={{0,136},{4,140},{8,128},{12,132},{16,152},{20,156},{24,144},{28,14... | collective-permute-start | bytes 49160 | tf_op jit(solution)/shard_map/ppermute | solution.py:124
  145.9 38.6 %collective-permute-start.16 = (f32[1024,64]{1,0:T(8,128)}, f32[1024,64]{1,0:T(8,128)S(1)}, u32[]{:S(2)}, u32[]{:S(2)}) collective-permute-start(f32[1024,64]{1,0:T(8,128)} %get-tuple-element.72), channel_id=1, source_target_pairs={{0,32},{4,36},{8,40},{12,44},{16,48},{20,52},{24,56},{28,60},{32,0... | collective-permute-start | bytes 786440 | tf_op jit(solution)/shard_map/ppermute | solution.py:130
  147.2 38.6 %collective-permute-start.17 = (f32[1024,64]{1,0:T(8,128)}, f32[1024,64]{1,0:T(8,128)S(1)}, u32[]{:S(2)}, u32[]{:S(2)}) collective-permute-start(f32[1024,64]{1,0:T(8,128)} %get-tuple-element.72), channel_id=1, source_target_pairs={{0,64},{4,68},{8,72},{12,76},{16,80},{20,84},{24,88},{28,92},{32,9... | collective-permute-start | bytes 786440 | tf_op jit(solution)/shard_map/ppermute | solution.py:130
  158.4 46.2 %collective-permute-start.1 = (f32[64,48]{1,0:T(8,128)}, f32[64,48]{1,0:T(8,128)S(1)}, u32[]{:S(2)}, u32[]{:S(2)}) collective-permute-start(f32[64,48]{1,0:T(8,128)} %get-tuple-element.40), channel_id=1, source_target_pairs={{0,1},{1,2},{2,3},{4,5},{5,6},{6,7},{8,9},{9,10},{10,11},{12,13},{... | collective-permute-start | bytes 36872 | tf_op jit(solution)/shard_map/ppermute | solution.py:21
  170.2 34.4 %collective-permute-start.4 = (f32[64,48]{1,0:T(8,128)}, f32[64,48]{1,0:T(8,128)S(1)}, u32[]{:S(2)}, u32[]{:S(2)}) collective-permute-start(f32[64,48]{1,0:T(8,128)} %get-tuple-element.34), channel_id=1, source_target_pairs={{1,0},{2,1},{3,2},{5,4},{6,5},{7,6},{9,8},{10,9},{11,10},{13,12},{... | collective-permute-start | bytes 36872 | tf_op jit(solution)/shard_map/ppermute | solution.py:21
  176.0 28.6 %collective-permute-start.5 = (f32[64,48]{1,0:T(8,128)}, f32[64,48]{1,0:T(8,128)S(1)}, u32[]{:S(2)}, u32[]{:S(2)}) collective-permute-start(f32[64,48]{1,0:T(8,128)} %get-tuple-element.33), channel_id=1, source_target_pairs={{0,1},{1,2},{2,3},{4,5},{5,6},{6,7},{8,9},{9,10},{10,11},{12,13},{... | collective-permute-start | bytes 36872 | tf_op jit(solution)/shard_map/ppermute | solution.py:21
  184.5 12.9 %collective-permute-start.18 = (f32[1024,64]{1,0:T(8,128)}, f32[1024,64]{1,0:T(8,128)S(1)}, u32[]{:S(2)}, u32[]{:S(2)}) collective-permute-start(f32[1024,64]{1,0:T(8,128)} %get-tuple-element.72), channel_id=1, source_target_pairs={{0,96},{4,100},{8,104},{12,108},{16,112},{20,116},{24,120},{28,124... | collective-permute-start | bytes 786440 | tf_op jit(solution)/shard_map/ppermute | solution.py:130
  201.6 50.5 %collective-permute-start.19 = (f32[4096,64]{0,1:T(8,128)}, f32[4096,64]{0,1:T(8,128)}, u32[]{:S(2)}, u32[]{:S(2)}) collective-permute-start(f32[4096,64]{0,1:T(8,128)} %copy.694), channel_id=1, source_target_pairs={{0,4},{4,0},{8,12},{12,8},{16,20},{20,16},{24,28},{28,24},{32,36},... | collective-permute-start | bytes 3145736 | tf_op jit(solution)/shard_map/ppermute | solution.py:130
  281.3 13.4 %collective-permute-start.20 = (f32[64,48]{1,0:T(8,128)S(1)}, f32[64,48]{1,0:T(8,128)S(1)}, u32[]{:S(2)}, u32[]{:S(2)}) collective-permute-start(f32[64,48]{1,0:T(8,128)S(1)} %bitcast.241), channel_id=1, source_target_pairs={{1,0},{2,1},{3,2},{5,4},{6,5},{7,6},{9,8},{10,9},{11,10},{13,12},{... | collective-permute-start | bytes 36872 | tf_op jit(solution)/shard_map/ppermute | solution.py:21
  291.4 9.6 %collective-permute-start.22 = (f32[64,128]{1,0:T(8,128)S(1)}, f32[64,128]{1,0:T(8,128)S(1)}, u32[]{:S(2)}, u32[]{:S(2)}) collective-permute-start(f32[64,128]{1,0:T(8,128)S(1)} %bitcast.243), channel_id=1, source_target_pairs={{4,0},{8,4},{12,8},{16,12},{20,16},{24,20},{28,24},{32,28},{36,32}... | collective-permute-start | bytes 98312 | tf_op jit(solution)/shard_map/ppermute | solution.py:21
  301.2 16.9 %collective-permute-start.25 = (f32[64,64]{1,0:T(8,128)S(1)}, f32[64,64]{1,0:T(8,128)S(1)}, u32[]{:S(2)}, u32[]{:S(2)}) collective-permute-start(f32[64,64]{1,0:T(8,128)S(1)} %fusion.11), channel_id=1, source_target_pairs={{0,128},{4,132},{8,136},{12,140},{16,144},{20,148},{24,152},{28,15... | collective-permute-start | bytes 49160 | tf_op jit(solution)/shard_map/ppermute | solution.py:124
  311.8 20.6 %collective-permute-start.23 = (f32[64,128]{1,0:T(8,128)S(1)}, f32[64,128]{1,0:T(8,128)S(1)}, u32[]{:S(2)}, u32[]{:S(2)}) collective-permute-start(f32[64,128]{1,0:T(8,128)S(1)} %bitcast.242), channel_id=1, source_target_pairs={{0,4},{4,8},{8,12},{12,16},{16,20},{20,24},{24,28},{28,32},{32,36}... | collective-permute-start | bytes 98312 | tf_op jit(solution)/shard_map/ppermute | solution.py:21
  324.6 20.0 %collective-permute-start.29 = (f32[256,64]{1,0:T(8,128)}, f32[256,64]{1,0:T(8,128)}, u32[]{:S(2)}, u32[]{:S(2)}) collective-permute-start(f32[256,64]{1,0:T(8,128)} %get-tuple-element.86), channel_id=1, source_target_pairs={{0,1},{1,0},{2,3},{3,2},{4,5},{5,4},{6,7},{7,6},{8,9},{9,8},{10,11... | collective-permute-start | bytes 196616 | tf_op jit(solution)/shard_map/ppermute | solution.py:130
  330.4 22.2 %collective-permute-start.21 = (f32[64,48]{1,0:T(8,128)S(1)}, f32[64,48]{1,0:T(8,128)S(1)}, u32[]{:S(2)}, u32[]{:S(2)}) collective-permute-start(f32[64,48]{1,0:T(8,128)S(1)} %bitcast.240), channel_id=1, source_target_pairs={{0,1},{1,2},{2,3},{4,5},{5,6},{6,7},{8,9},{9,10},{10,11},{12,13},{... | collective-permute-start | bytes 36872 | tf_op jit(solution)/shard_map/ppermute | solution.py:21
  350.5 35.0 %collective-permute-start.32 = (f32[1024,64]{1,0:T(8,128)}, f32[1024,64]{1,0:T(8,128)S(1)}, u32[]{:S(2)}, u32[]{:S(2)}) collective-permute-start(f32[1024,64]{1,0:T(8,128)} %get-tuple-element.63), channel_id=1, source_target_pairs={{0,32},{4,36},{8,40},{12,44},{16,48},{20,52},{24,56},{28,60},{32,0... | collective-permute-start | bytes 786440 | tf_op jit(solution)/shard_map/ppermute | solution.py:130
  350.5 36.0 %collective-permute-start.33 = (f32[1024,64]{1,0:T(8,128)}, f32[1024,64]{1,0:T(8,128)S(1)}, u32[]{:S(2)}, u32[]{:S(2)}) collective-permute-start(f32[1024,64]{1,0:T(8,128)} %get-tuple-element.63), channel_id=1, source_target_pairs={{0,64},{4,68},{8,72},{12,76},{16,80},{20,84},{24,88},{28,92},{32,9... | collective-permute-start | bytes 786440 | tf_op jit(solution)/shard_map/ppermute | solution.py:130
  383.7 13.0 %collective-permute-start.34 = (f32[1024,64]{1,0:T(8,128)}, f32[1024,64]{1,0:T(8,128)S(1)}, u32[]{:S(2)}, u32[]{:S(2)}) collective-permute-start(f32[1024,64]{1,0:T(8,128)} %get-tuple-element.63), channel_id=1, source_target_pairs={{0,96},{4,100},{8,104},{12,108},{16,112},{20,116},{24,120},{28,124... | collective-permute-start | bytes 786440 | tf_op jit(solution)/shard_map/ppermute | solution.py:130
  400.9 23.7 %collective-permute-start.35 = (f32[4096,64]{0,1:T(8,128)}, f32[4096,64]{0,1:T(8,128)}, u32[]{:S(2)}, u32[]{:S(2)}) collective-permute-start(f32[4096,64]{0,1:T(8,128)} %copy.722), channel_id=1, source_target_pairs={{0,4},{4,0},{8,12},{12,8},{16,20},{20,16},{24,28},{28,24},{32,36},... | collective-permute-start | bytes 3145736 | tf_op jit(solution)/shard_map/ppermute | solution.py:130
  (37 other events, 448.0 us)
